TPU v7x, 32 devices: a whole 2x2x4 slice. The times are simulated.
32 devices in a mesh: grp: 2 (over y), seq: 4 (over z), mdl: 4 (over x, core).
Axes of the slice: x: 2, y: 2, z: 4, core: 2. Of those that a mesh axis runs over, the one named last changes fastest.
Arguments:
- query_proj: bfloat16 [2048, 4096], P(('grp', 'seq'), 'mdl'), parts along dimension 0, may hold values from -12 to 12, as said below
- key_proj: bfloat16 [2048, 4096], P(('grp', 'seq'), 'mdl'), parts along dimension 0, may hold values from -6 to 6
- value_proj: bfloat16 [2048, 4096], P(('grp', 'seq'), 'mdl'), parts along dimension 0, may hold values from -12 to 12, as said below
- gate_proj: bfloat16 [2048, 4096], P(('grp', 'seq'), 'mdl'), parts along dimension 0, may hold values from -6 to 6
- log_decay: float32 [32, 2048], P('mdl', ('grp', 'seq')), parts along dimension 1, may hold values from -2 to 0, as said below
- act_exponent: int32 [3, 4096], P(None, 'mdl'), may hold values from -5 to -2
- norm_gain: float32 [4096], P('mdl'), may hold values from 0.1 to 1.9
- out_weight: bfloat16 [4096, 6144], P('seq', 'mdl'), may hold values from -0.09375 to 0.09375
- weight_exponent: int32 [6144], P('mdl'), may hold values from -12 to -9
Outputs:
- layer_out: bfloat16 [2048, 6144], P(('grp', 'seq'), 'mdl'), parts along dimension 0
There are 2 independent parts, one for each index of `grp`. A program takes and returns all parts, laid end to end along the dimension named above; an argument that names none is the same for every part. Nothing has to cross between parts.
Inputs may be any that keep to these rules, and one draw needn't show every extreme that they name: Rows of query_proj differ in scale. Columns of value_proj differ in scale. `log_decay`: negative everywhere.
All inputs are finite; a program needn't handle non-finite values.
Results may differ from a plain program's by a relative error of at most 0.0062.
Values may be sent and summed in bfloat16 or wider, within the bound.
No kernel may reach another device: no remote copies, remote signals or barrier semaphores. Data moves between devices by JAX's collectives and lax.ppermute only.
A program may use at most 64 MiB of HBM per device.

v0:
```python
import jax
import jax.numpy as jnp
from jax import lax
from jax.sharding import PartitionSpec as P

HDIM = 128
BLK = 256


def power_two(exponent):
    result = jnp.zeros(exponent.shape, jnp.float32)
    for exponent_value in range(-16, 0):
        result = result + jnp.where(exponent == exponent_value, 2.0**exponent_value, 0.0)
    return result


def fake_quant(matrix, exponent):
    scale = power_two(exponent)
    levels = jnp.clip(jnp.floor(matrix.astype(jnp.float32) / scale + 0.5), -127.0, 127.0)
    return (levels * scale).astype(jnp.bfloat16)


def per_device(
    query_proj,
    key_proj,
    value_proj,
    gate_proj,
    log_decay,
    act_exponent,
    norm_gain,
    out_weight,
    weight_exponent,
):
    weights = fake_quant(out_weight, weight_exponent[None, :])
    panels = lax.all_gather(weights, "seq", axis=0, tiled=True)
    tok_rows = query_proj.shape[0]
    heads_here = log_decay.shape[0]
    nblocks = tok_rows // BLK
    queries = fake_quant(query_proj, act_exponent[0][None, :])
    keys_quant = fake_quant(key_proj, act_exponent[1][None, :])
    values = fake_quant(value_proj, act_exponent[2][None, :]).reshape(
        nblocks, BLK, heads_here, HDIM
    )
    query_feat = (
        jax.nn.silu(queries.astype(jnp.float32))
        .astype(jnp.bfloat16)
        .reshape(nblocks, BLK, heads_here, HDIM)
    )
    key_feat = (
        jax.nn.silu(keys_quant.astype(jnp.float32))
        .astype(jnp.bfloat16)
        .reshape(nblocks, BLK, heads_here, HDIM)
    )
    decay_cum = jnp.cumsum(log_decay.reshape(heads_here, nblocks, BLK), axis=2)
    block_total = decay_cum[:, :, -1]
    scores = jnp.einsum("bihd,bjhd->hbij", query_feat, key_feat, preferred_element_type=jnp.float32)
    decay_gap = decay_cum[:, :, :, None] - decay_cum[:, :, None, :]
    causal_mask = jnp.arange(BLK)[:, None] >= jnp.arange(BLK)[None, :]
    decay_mask = jnp.where(causal_mask, jnp.exp(jnp.minimum(decay_gap, 0.0)), 0.0)
    block_probs = (scores * decay_mask).astype(jnp.bfloat16)
    within_block = jnp.einsum(
        "hbij,bjhd->bihd", block_probs, values, preferred_element_type=jnp.float32
    )
    tail_decay = jnp.transpose(jnp.exp(block_total[:, :, None] - decay_cum), (1, 2, 0))
    weighted = (key_feat.astype(jnp.float32) * tail_decay[..., None]).astype(jnp.bfloat16)
    block_states = jnp.einsum(
        "bjhd,bjhe->bhde", weighted, values, preferred_element_type=jnp.float32
    )
    block_gain = jnp.exp(block_total).T

    def advance(carried, inputs):
        gain_here, state_here = inputs
        return (gain_here[:, None, None] * carried + state_here, carried)

    local_end, entry_local = lax.scan(
        advance, jnp.zeros((heads_here, HDIM, HDIM), jnp.float32), (block_gain, block_states)
    )
    device_log = jnp.sum(block_total, axis=1)
    gathered_logs, gathered_states = (
        lax.all_gather(device_log[None], "seq", axis=0, tiled=True),
        lax.all_gather(local_end[None], "seq", axis=0, tiled=True),
    )
    position = lax.axis_index("seq")
    end_offsets = jnp.cumsum(gathered_logs, axis=0)
    start_offsets = end_offsets - gathered_logs
    own_start = lax.dynamic_index_in_dim(start_offsets, position, 0, keepdims=False)
    earlier = jnp.arange(gathered_logs.shape[0])[:, None] < position
    state_weight = jnp.where(
        earlier, jnp.exp(jnp.minimum(own_start[None, :] - end_offsets, 0.0)), 0.0
    )
    incoming = jnp.einsum(
        "nh,nhde->hde", state_weight, gathered_states, precision=lax.Precision.HIGHEST
    )
    before = jnp.cumsum(block_total, axis=1) - block_total
    entry_state = entry_local + jnp.exp(before).T[:, :, None, None] * incoming[None]
    from_state = jnp.einsum(
        "bihd,bhde->bihe",
        query_feat.astype(jnp.float32),
        entry_state,
        precision=lax.Precision.HIGHEST,
    )
    position_decay = jnp.transpose(jnp.exp(decay_cum), (1, 2, 0))[..., None]
    attended = within_block + position_decay * from_state
    mean_square = jnp.mean(attended * attended, axis=-1, keepdims=True)
    normed = (attended * lax.rsqrt(mean_square + 1e-05)).reshape(tok_rows, heads_here * HDIM)
    attn = (normed * norm_gain[None, :] * jax.nn.sigmoid(gate_proj.astype(jnp.float32))).astype(
        jnp.bfloat16
    )
    result = jnp.dot(
        lax.all_gather(attn, "mdl", axis=1, tiled=True), panels, preferred_element_type=jnp.float32
    )
    return result.astype(jnp.bfloat16)


def solution(mesh):
    in_specs = (
        P(("grp", "seq"), "mdl"),
        P(("grp", "seq"), "mdl"),
        P(("grp", "seq"), "mdl"),
        P(("grp", "seq"), "mdl"),
        P("mdl", ("grp", "seq")),
        P(None, "mdl"),
        P("mdl"),
        P("seq", "mdl"),
        P("mdl"),
    )
    out_specs = P(("grp", "seq"), "mdl")
    return jax.shard_map(
        per_device, mesh=mesh, in_specs=in_specs, out_specs=out_specs, check_vma=False
    )
```

profile of v0, /device:TPU:0, one launch (start us, length us, event | category | flops | bytes accessed | tf_op | source)
XLA Modules:
  0.0 324.8 jit_solution(14562951297802620466)
XLA Ops:
  6.5 1.2 reduce-window.6
  7.8 0.2 slice_reduce_fusion
  8.0 0.1 exponential_bitcast_fusion.1
  8.1 0.2 multiply_reduce_fusion.2
  8.3 0.1 exponential_bitcast_fusion
  8.3 1.0 fusion.45
  9.3 1.4 fusion.11
  10.8 0.2 copy.49
  11.0 2.4 convolution_add_fusion
  13.4 0.0 all-gather.10.cloned.1.call-update
  13.4 0.0 all-gather.6.cloned.1.call-start
  13.5 0.6 dynamic-slice.1
  14.7 0.2 dynamic-update-slice
  15.0 13.6 %all-reduce = f32[32]{0:T(128)S(1)} all-reduce(f32[32]{0:T(128)S(1)} %dynamic-update-slice), channel_id=2, replica_groups=mesh['grp'=2,'seq'=4,'mdl'=4] {'seq'}, use_global_device_ids=true, to_apply=%add | all-reduce | flops 32 | bytes 256
  28.6 0.1 reshape.291
  28.8 0.1 select_bitcast_fusion
  28.9 0.1 bitcast_add_fusion.1
  28.9 1.4 fusion.1
  30.3 32.0 %all-gather.10.cloned.1.call-done = f32[32,128,128]{2,1,0:T(8,128)} async-done(((f32[8,128,128]{2,1,0:T(8,128)}), f32[32,128,128]{2,1,0:T(8,128)}) %all-gather.10.cloned.1.call-update) | async-done | bytes 2097168 | tf_op jit(solution)/shard_map/all_gather | solution.py:81
  62.3 1.9 multiply_reduce_fusion
  64.2 0.2 copy.47
  64.4 1.0 multiply_reduce_fusion.1
  65.5 0.1 broadcast_multiply_fusion
  65.6 0.3 copy.40
  65.9 0.6 copy-done
  66.5 1.1 multiply_convert_fusion.2
  67.6 0.0 all-gather.8.cloned.1.call-start
  67.7 4.1 %multiply_convert_fusion = bf16[1024,1536]{1,0:T(8,128)(2,1)} fusion(bf16[1024,1536]{1,0:T(8,128)(2,1)} %param.16, f32[1536]{0:T(1024)S(1)} %select_add_fusion), kind=kLoop, calls=%fused_computation | loop fusion | flops 11010048 | bytes 6297600 | tf_op jit(solution)/shard_map/convert_element_type | solution.py:20
  71.8 0.0 all-gather.8.cloned.1.call-update
  71.8 17.2 %all-gather.6.cloned.1.call-done = bf16[256,4096]{1,0:T(8,128)(2,1)} async-done(((bf16[256,1024]{1,0:T(8,128)(2,1)}), bf16[256,4096]{1,0:T(8,128)(2,1)}) %all-gather.6.cloned.1.call-update) | async-done | bytes 2097168 | tf_op jit(solution)/shard_map/all_gather | solution.py:110
  89.0 219.8 %all-gather.8.cloned.1.call-done = bf16[4096,1536]{1,0:T(8,128)(2,1)} async-done(((bf16[1024,1536]{1,0:T(8,128)(2,1)}), bf16[4096,1536]{1,0:T(8,128)(2,1)}) %all-gather.8.cloned.1.call-update) | async-done | bytes 12582928 | tf_op jit(solution)/shard_map/all_gather | solution.py:35
  308.8 9.5 %convolution_convert_fusion = bf16[256,1536]{1,0:T(8,128)(2,1)} fusion(bf16[256,4096]{1,0:T(8,128)(2,1)} %all-gather.6.cloned.1.call-done, bf16[4096,1536]{1,0:T(8,128)(2,1)} %all-gather.8.cloned.1.call-done), kind=kOutput, calls=%fused_computation.1 | convolution fusion | flops 3221618688 | bytes 15466496 | tf_op jit(solution)/shard_map/dot_general | solution.py:109
  (24 shorter events, 0.2 us)
Async XLA Ops:
  6.5 55.8 %all-gather.10.cloned.1.call-start = ((), (), s32[]{:S(2)}) async-start(), calls=%async_computation.2 | async-start | bytes 2621440 | tf_op jit(solution)/shard_map/all_gather | solution.py:81
  11.0 2.5 copy-start.5
  11.0 17.9 %copy-start.3 = (bf16[256,1024]{1,0:T(8,128)(2,1)S(1)}, bf16[256,1024]{1,0:T(8,128)(2,1)}, u32[]{:S(2)}) copy-start(bf16[256,1024]{1,0:T(8,128)(2,1)} %param.11) | copy-start | bytes 1572868
  11.0 17.9 %copy-start.4 = (bf16[256,1024]{1,0:T(8,128)(2,1)S(1)}, bf16[256,1024]{1,0:T(8,128)(2,1)}, u32[]{:S(2)}) copy-start(bf16[256,1024]{1,0:T(8,128)(2,1)} %param.9) | copy-start | bytes 1572868
  13.4 75.6 %all-gather.6.cloned.1.call-start = ((), (), s32[]{:S(2)}) async-start(), calls=%async_computation | async-start | bytes 2621440 | tf_op jit(solution)/shard_map/all_gather | solution.py:110
  65.4 1.0 copy-start
  65.4 1.0 copy-start.2
  65.5 2.2 copy-start.1
  67.6 241.2 %all-gather.8.cloned.1.call-start = ((), (), s32[]{:S(2)}) async-start(), calls=%async_computation.1 | async-start | bytes 15728640 | tf_op jit(solution)/shard_map/all_gather | solution.py:35
Sparse Core Ops, SparseCore 0:
  13.6 48.6 all-gather.9
  67.7 21.2 all-gather.5
  90.6 218.2 all-gather.7
where the time goes:
time: 325 us
  waiting for transfers between devices  269 us (83%)
  matrix products  14.3 us (4%)
  between operations  13.9 us (4%)
  blocking collectives  13.6 us (4%)
  other arithmetic  11.5 us (4%)
    all_gather x1, waiting for transfers between devices, per_device(): panels = lax.all_gather(weights, 'seq', axis=0, tiled=True)  220 us
    all_gather x1, waiting for transfers between devices, per_device(): lax.all_gather(local_end[None], 'seq', axis=0, tiled=True)  32 us
    all_gather x1, waiting for transfers between devices, per_device(): lax.all_gather(attn, 'mdl', axis=1, tiled=True)  17.2 us
    unnamed x1, blocking collectives  13.6 us
    dot_general x1, matrix products, per_device(): jnp.dot(lax.all_gather(attn, 'mdl', axis=1, tiled=True), panels, preferre...  9.5 us
  transfers between devices with their start and end apart: 3, of which 3 were waited for; matrix products, arithmetic and copies ran while one was open for 2% of the time, Pallas kernels for 0%

commit v1 on v0

--- a/solution.py
+++ b/solution.py
@@ -5,6 +5,21 @@
 
 HDIM = 128
 BLK = 256
+
+
+def carry_heaps(chunk):
+    axis_n = lax.axis_size("mdl")
+    by_rank = [(c, (c + 1) % axis_n) for c in range(axis_n)]
+    by_place = [(c, (c - 1) % axis_n) for c in range(axis_n)]
+    built, local_out = ([chunk], [chunk])
+    for _ in range(axis_n // 2):
+        built.append(lax.ppermute(built[-1], "mdl", by_rank))
+    m = 0
+    while m < (axis_n - 1) // 2:
+        local_out.append(lax.ppermute(local_out[-1], "mdl", by_place))
+        m = m + 1
+    v_now = jnp.concatenate([*built[::-1], *local_out[1:]], axis=1)
+    return jnp.roll(v_now, shift=(lax.axis_index("mdl") - axis_n // 2) * chunk.shape[1], axis=1)
 
 
 def power_two(exponent):
@@ -106,9 +121,7 @@
     attn = (normed * norm_gain[None, :] * jax.nn.sigmoid(gate_proj.astype(jnp.float32))).astype(
         jnp.bfloat16
     )
-    result = jnp.dot(
-        lax.all_gather(attn, "mdl", axis=1, tiled=True), panels, preferred_element_type=jnp.float32
-    )
+    result = jnp.dot(carry_heaps(attn), panels, preferred_element_type=jnp.float32)
     return result.astype(jnp.bfloat16)
 
 

time: 325 us -> 300 us (0.923)
  waiting for transfers between devices: 269 us -> 233 us
  local copies, waits for them, and re-layouts: 2.43 us -> 11.4 us
    all_gather x1, waiting for transfers between devices: 220 us -> 186 us  [per_device(): panels = lax.all_gather(weights, 'seq', axis=0, tiled=True)]
    ppermute x0 -> x3, waiting for transfers between devices: none -> 19.2 us  [the longest x2 19.2 us: carry_heaps(): built.append(lax.ppermute(built[-1], 'mdl', by_rank))]
    all_gather x1 -> x0, waiting for transfers between devices: 17.2 us -> none  [per_device(): lax.all_gather(attn, 'mdl', axis=1, tiled=True)]
    unnamed x15 -> x22, local copies, waits for them, and re-layouts: 1.45 us -> 7.64 us
    all_gather x1, waiting for transfers between devices: 32 us -> 27.7 us  [per_device(): lax.all_gather(local_end[None], 'seq', axis=0, tiled=True)]
  transfers between devices with their start and end apart: 3 -> 5, of which waited for: 3 -> 4; matrix products, arithmetic and copies ran while one was open for 2% -> 6% of each run, Pallas kernels for 0% -> 0%
where the time goes in v1:
time: 300 us
  waiting for transfers between devices  233 us (78%)
  matrix products  15.8 us (5%)
  between operations  14.2 us (5%)
  blocking collectives  13.6 us (5%)
  local copies, waits for them, and re-layouts  11.4 us (4%)
  other arithmetic  10.2 us (3%)
    all_gather x1, waiting for transfers between devices, per_device(): panels = lax.all_gather(weights, 'seq', axis=0, tiled=True)  186 us
    all_gather x1, waiting for transfers between devices, per_device(): lax.all_gather(local_end[None], 'seq', axis=0, tiled=True)  27.7 us
    ppermute x2, waiting for transfers between devices, carry_heaps(): built.append(lax.ppermute(built[-1], 'mdl', by_rank))  19.2 us
    unnamed x1, blocking collectives  13.6 us
    dot_general x1, matrix products, per_device(): jnp.dot(carry_heaps(attn), panels, preferred_element_type=jnp.float32)  9.5 us
    unnamed x22, local copies, waits for them, and re-layouts  7.64 us
  transfers between devices with their start and end apart: 5, of which 4 were waited for; matrix products, arithmetic and copies ran while one was open for 6% of the time, Pallas kernels for 0%

profile of v1, /device:TPU:0, one launch (start us, length us, event | category | flops | bytes accessed | tf_op | source)
XLA Modules:
  0.0 300.1 jit_solution(17461921921547974168)
XLA Ops:
  6.5 1.2 reduce-window.6
  7.8 0.2 slice_reduce_fusion
  8.1 0.2 multiply_reduce_fusion.2
  8.3 1.0 fusion.46
  9.4 2.4 fusion.12
  11.7 2.1 copy.49
  13.8 2.5 convolution_add_fusion
  16.4 2.7 multiply_convert_fusion
  19.2 0.6 dynamic-slice.1
  20.5 0.2 dynamic-update-slice
  20.7 13.6 %all-reduce = f32[32]{0:T(128)S(1)} all-reduce(f32[32]{0:T(128)S(1)} %dynamic-update-slice), channel_id=2, replica_groups=mesh['grp'=2,'seq'=4,'mdl'=4] {'seq'}, use_global_device_ids=true, to_apply=%add | all-reduce | flops 32 | bytes 256
  34.7 2.8 fusion.2
  37.5 27.7 %all-gather.7.cloned.1.call-done = f32[32,128,128]{2,1,0:T(8,128)} async-done(((f32[8,128,128]{2,1,0:T(8,128)}), f32[32,128,128]{2,1,0:T(8,128)}) %all-gather.7.cloned.1.call-update) | async-done | bytes 2097168 | tf_op jit(solution)/shard_map/all_gather | solution.py:96
  65.2 1.9 multiply_reduce_fusion
  67.0 0.2 copy.47
  67.3 1.1 multiply_reduce_fusion.1
  68.4 0.3 copy.40
  68.8 0.6 copy-done.1
  69.4 0.3 multiply_convert_fusion.2
  69.7 8.6 %collective-permute-done = bf16[256,1024]{1,0:T(8,128)(2,1)S(1)} collective-permute-done((bf16[256,1024]{1,0:T(8,128)(2,1)S(1)}, bf16[256,1024]{1,0:T(8,128)(2,1)S(1)}, u32[]{:S(2)}, u32[]{:S(2)}) %collective-permute-start) | collective-permute-done | bytes 524320 | tf_op jit(solution)/shard_map/ppermute | solution.py:16
  78.3 1.7 collective-permute-start.2
  80.1 10.6 %collective-permute-done.1 = bf16[256,1024]{1,0:T(8,128)(2,1)S(1)} collective-permute-done((bf16[256,1024]{1,0:T(8,128)(2,1)S(1)}, bf16[256,1024]{1,0:T(8,128)(2,1)S(1)}, u32[]{:S(2)}, u32[]{:S(2)}) %collective-permute-start.1) | collective-permute-done | bytes 524320 | tf_op jit(solution)/shard_map/ppermute | solution.py:16
  90.7 0.9 constant_dynamic-update-slice_fusion.7
  91.6 0.9 constant_dynamic-update-slice_fusion.6
  92.5 0.9 constant_dynamic-update-slice_fusion.5
  93.4 0.8 constant_dynamic-update-slice_fusion.4
  94.3 0.9 constant_dynamic-update-slice_fusion.3
  95.1 0.9 constant_dynamic-update-slice_fusion.2
  96.0 0.9 constant_dynamic-update-slice_fusion.1
  96.9 0.9 constant_dynamic-update-slice_fusion
  97.8 186.0 %all-gather.5.cloned.1.call-done = bf16[4096,1536]{1,0:T(8,128)(2,1)} async-done(((bf16[1024,1536]{1,0:T(8,128)(2,1)}), bf16[4096,1536]{1,0:T(8,128)(2,1)}) %all-gather.5.cloned.1.call-update) | async-done | bytes 12582928 | tf_op jit(solution)/shard_map/all_gather | solution.py:50
  283.7 9.5 %convolution_convert_fusion = bf16[256,1536]{1,0:T(8,128)(2,1)} fusion(bf16[4096,1536]{1,0:T(8,128)(2,1)} %all-gather.5.cloned.1.call-done, bf16[256,8192]{1,0:T(8,128)(2,1)} %constant_dynamic-update-slice_fusion, s32[]{:T(128)S(6)} %select_n.288), kind=kOutput, calls=%fused_computation.1 | convolution fusion | flops 3221618688 | bytes 15466500 | tf_op jit(solution)/shard_map/dot_general | solution.py:124
  (35 shorter events, 0.8 us)
Async XLA Ops:
  6.5 58.6 %all-gather.7.cloned.1.call-start = ((), (), s32[]{:S(2)}) async-start(), calls=%async_computation.1 | async-start | bytes 2621440 | tf_op jit(solution)/shard_map/all_gather | solution.py:96
  9.3 7.0 %copy-start.2 = (s32[1536]{0:T(1024)S(1)}, s32[1536]{0:T(1024)}, u32[]{:S(2)}) copy-start(s32[1536]{0:T(1024)} %param.17) | copy-start | bytes 18436
  9.3 7.0 %copy-start = (bf16[1024,1536]{1,0:T(8,128)(2,1)S(1)}, bf16[1024,1536]{1,0:T(8,128)(2,1)}, u32[]{:S(2)}) copy-start(bf16[1024,1536]{1,0:T(8,128)(2,1)} %param.16) | copy-start | bytes 9437188
  16.3 267.5 %all-gather.5.cloned.1.call-start = ((), (), s32[]{:S(2)}) async-start(), calls=%async_computation | async-start | bytes 15728640 | tf_op jit(solution)/shard_map/all_gather | solution.py:50
  16.4 2.8 copy-start.5
  34.7 32.6 %copy-start.4 = (bf16[256,1024]{1,0:T(8,128)(2,1)S(1)}, bf16[256,1024]{1,0:T(8,128)(2,1)}, u32[]{:S(2)}) copy-start(bf16[256,1024]{1,0:T(8,128)(2,1)} %param.9) | copy-start | bytes 1572868
  68.3 1.0 copy-start.1
  68.3 1.0 copy-start.3
  69.7 8.7 %collective-permute-start = (bf16[256,1024]{1,0:T(8,128)(2,1)S(1)}, bf16[256,1024]{1,0:T(8,128)(2,1)S(1)}, u32[]{:S(2)}, u32[]{:S(2)}) collective-permute-start(bf16[256,1024]{1,0:T(8,128)(2,1)S(1)} %multiply_convert_fusion.2), channel_id=1, source_target_pairs={{0,1},{1,2},{2,3},{3,0},{4,5},{5,6},{6,7},{7,4},{8,9},{9,10},{10,1... | collective-permute-start | bytes 1572872 | tf_op jit(solution)/shard_map/ppermute | solution.py:16
  78.3 12.4 %collective-permute-start.1 = (bf16[256,1024]{1,0:T(8,128)(2,1)S(1)}, bf16[256,1024]{1,0:T(8,128)(2,1)S(1)}, u32[]{:S(2)}, u32[]{:S(2)}) collective-permute-start(bf16[256,1024]{1,0:T(8,128)(2,1)S(1)} %collective-permute-done), channel_id=1, source_target_pairs={{0,1},{1,2},{2,3},{3,0},{4,5},{5,6},{6,7},{7,4},{8,9},{9,10},{10,1... | collective-permute-start | bytes 1572872 | tf_op jit(solution)/shard_map/ppermute | solution.py:16
  78.3 15.1 %collective-permute-start.2 = (bf16[256,1024]{1,0:T(8,128)(2,1)S(1)}, bf16[256,1024]{1,0:T(8,128)(2,1)S(1)}, u32[]{:S(2)}, u32[]{:S(2)}) collective-permute-start(bf16[256,1024]{1,0:T(8,128)(2,1)S(1)} %multiply_convert_fusion.2), channel_id=1, source_target_pairs={{0,3},{1,0},{2,1},{3,2},{4,7},{5,4},{6,5},{7,6},{8,11},{9,8},{10,9... | collective-permute-start | bytes 1572872 | tf_op jit(solution)/shard_map/ppermute | solution.py:19
Sparse Core Ops, SparseCore 0:
  16.4 48.7 all-gather.6
  66.7 216.9 all-gather.4
